TPU v7x, 128 devices: a whole 4x4x4 slice. The times are simulated.
128 devices in a mesh: fsdp: 32 (over z, y, core), fac: 4 (over x).
Axes of the slice: x: 4, y: 4, z: 4, core: 2. Of those that a mesh axis runs over, the one named last changes fastest.
Arguments:
- activations: bfloat16 [32768, 3072], P('fsdp'), may hold values from -6 to 6
- out_grads: bfloat16 [32768, 3072], P('fsdp', 'fac'), may hold values from -12 to 12
- token_ids: int32 [32768], P('fsdp'), may hold values from 0 to 32767
- forget_mask: int32 [32768], P('fsdp'), may hold values 0 or 1
- importance: float32 [32768], replicated, may hold values from 0.3 to 3
- in_inverse: bfloat16 [3072, 3072], P('fsdp'), may hold values from -1 to 3, as said below
- out_inverse: bfloat16 [3072, 3072], P(None, 'fac'), may hold values from -1 to 3, as said below
Outputs:
- newton_step: float32 [3072, 3072], P('fsdp', 'fac')
- residual: float32 [3072, 3072], P('fsdp', 'fac')
Inputs may be any that keep to these rules, and one draw needn't show every extreme that they name: `in_inverse`: symmetric and positive definite. `out_inverse`: symmetric and positive definite.
All inputs are finite; a program needn't handle non-finite values. No bound on the sum of `forget_mask` on one device may be relied on, other than what follows from the above.
Results may differ from a plain program's by a relative error of at most 0.03.
Values may be sent and summed in bfloat16 or wider, within the bound.
No kernel may reach another device: no remote copies, remote signals or barrier semaphores. Data moves between devices by JAX's collectives and lax.ppermute only.
A program may use at most 64 MiB of HBM per device.

v0:
```python
import math
import jax
import jax.numpy as jnp
from jax import lax
from jax.sharding import PartitionSpec as P

ITERS = 2
damping = 0.3


def add_columns(matrix, piece):
    return jnp.dot(matrix, piece, preferred_element_type=jnp.float32)


def transposed_term(matrix, right):
    return lax.dot_general(
        matrix, right, (((0,), (0,)), ((), ())), preferred_element_type=jnp.float32
    )


FSDP = ("pairs", "core")


def ring_product(piece, right):
    n = lax.axis_size("fac")
    me = lax.axis_index("fac")
    width = piece.shape[1]

    def right_block(k):
        return lax.dynamic_slice_in_dim(right, k % n * width, width, axis=0)

    total = add_columns(piece, right_block(me))
    ahead = piece
    behind = piece
    for step in range(1, n // 2 + 1):
        ahead = lax.ppermute(ahead, "fac", [(j, (j + 1) % n) for j in range(n)])
        total = total + add_columns(ahead, right_block(me - step))
        if 2 * step < n:
            behind = lax.ppermute(behind, "fac", [(j, (j - 1) % n) for j in range(n)])
            total = total + add_columns(behind, right_block(me + step))
    return total


def scatter_sum(partial):
    pairs, cores = (lax.axis_size("pairs"), lax.axis_size("core"))
    blocks = partial.reshape(pairs, cores, partial.shape[0] // (pairs * cores), partial.shape[1])
    on_chip = lax.all_to_all(blocks, "core", 1, 1, tiled=False)
    chip_sum = jnp.sum(on_chip.astype(jnp.float32), axis=1).astype(jnp.bfloat16)
    received = lax.all_to_all(chip_sum, "pairs", 0, 0, tiled=False)
    return lax.optimization_barrier(jnp.sum(received.astype(jnp.float32), axis=0))


def global_sums(*partials):
    devices = lax.axis_size("pairs") * lax.axis_size("core") * lax.axis_size("fac")
    stacked = jnp.broadcast_to(jnp.stack(partials)[None, :], (devices, len(partials)))
    received = lax.all_to_all(stacked, FSDP + ("fac",), 0, 0, tiled=True)
    total = jnp.sum(received, axis=0)
    return tuple((total[i] for i in range(len(partials))))


def body(activations, out_grads, token_ids, forget_mask, importance, in_inverse, out_inverse):
    tok_rows, d_in = activations.shape
    total = tok_rows * lax.axis_size("pairs") * lax.axis_size("core")
    keep = 1.0 - forget_mask.astype(jnp.float32)
    weights = importance[token_ids] * keep / total
    forget_grads = out_grads * forget_mask.astype(jnp.bfloat16)[:, None]
    grad_scale = 1.0 / math.sqrt(total)
    gradient = scatter_sum(
        (transposed_term(activations, forget_grads) * grad_scale).astype(jnp.bfloat16)
    )

    def gather_rows(matrix):
        return lax.all_gather(matrix.astype(jnp.bfloat16), FSDP, axis=0, tiled=True)

    def precondition(gathered):
        mixed = add_columns(in_inverse, gathered)
        mixed_low = mixed.astype(jnp.bfloat16)
        return jnp.dot(
            lax.all_gather(mixed_low, "fac", axis=1, tiled=True),
            out_inverse,
            preferred_element_type=jnp.float32,
        )

    def inner_part(left, right):
        return jnp.sum(left * right)

    d_out_part = out_inverse.shape[1]
    in_cols = lax.all_gather(
        lax.dynamic_slice_in_dim(
            in_inverse, lax.axis_index("fac") * d_out_part, d_out_part, axis=1
        ),
        FSDP,
        axis=0,
        tiled=True,
    )
    gradient, in_cols = lax.optimization_barrier((gradient, in_cols))
    residual = -gradient
    residual_rows = gather_rows(residual)
    gram_cols = d_in // lax.axis_size("fac")
    own_cols = lax.dynamic_slice_in_dim(
        activations, lax.axis_index("fac") * gram_cols, gram_cols, axis=1
    )
    weighted = (own_cols * weights[:, None]).astype(jnp.bfloat16)
    half = gram_cols // 2
    gram_first = transposed_term(activations, weighted[:, :half]).astype(jnp.bfloat16)
    gram_second = transposed_term(activations, weighted[:, half:]).astype(jnp.bfloat16)
    residual_rows, first_rows = lax.optimization_barrier((residual_rows, scatter_sum(gram_first)))
    precond = precondition(residual_rows)
    gram_own = jnp.concatenate([first_rows, scatter_sum(gram_second)], axis=1)
    gram_rows = lax.all_gather(gram_own.astype(jnp.bfloat16), "fac", axis=1, tiled=True)

    def curvature(matrix):
        return add_columns(gram_rows, gather_rows(matrix)) + damping * matrix

    direction = precond
    image = curvature(direction)
    image_rows = gather_rows(image)
    inner_now, energy = global_sums(inner_part(residual, precond), inner_part(direction, image))
    gram_inverse = lax.all_gather(
        add_columns(gram_rows, in_cols).astype(jnp.bfloat16), "fac", axis=1, tiled=True
    )
    alpha = inner_now / energy
    newton_step = alpha * direction
    residual = residual - alpha * image
    next_rows = (residual_rows.astype(jnp.float32) - alpha * image_rows.astype(jnp.float32)).astype(
        jnp.bfloat16
    )
    rows = in_inverse.shape[0]
    left = jnp.concatenate([in_inverse, gram_inverse], axis=0)
    both = add_columns(left, next_rows).astype(jnp.bfloat16)
    both_out = ring_product(both, out_inverse)
    precond = both_out[:rows]
    precond_image = both_out[rows:] + damping * precond
    inner_next, z_hz, z_hd, d_hz = global_sums(
        inner_part(residual, precond),
        inner_part(precond, precond_image),
        inner_part(precond, image),
        inner_part(direction, precond_image),
    )
    beta = inner_next / inner_now
    direction = precond + beta * direction
    image = precond_image + beta * image
    energy = z_hz + beta * (z_hd + d_hz) + beta * beta * energy
    alpha = inner_next / energy
    newton_step = newton_step + alpha * direction
    residual = residual - alpha * image
    return (newton_step, residual)


def solution(mesh):
    cores = 2
    split = jax.sharding.Mesh(
        mesh.devices.reshape(mesh.shape["fsdp"] // cores, cores, mesh.shape["fac"]),
        ("pairs", "core", "fac"),
    )
    placed = (P(FSDP, None), P(FSDP, "fac"), P(FSDP), P(FSDP), P(), P(FSDP, None), P(None, "fac"))
    return jax.shard_map(
        body,
        mesh=split,
        in_specs=placed,
        out_specs=(P(FSDP, "fac"), P(FSDP, "fac")),
        check_vma=False,
    )
```

profile of v0, /device:TPU:1, one launch (start us, length us, event | category | flops | bytes accessed | tf_op | source)
XLA Modules:
  0.0 333.9 jit_solution(15328082240654221681)
XLA Ops:
  7.2 1.6 constant_dynamic-slice_fusion
  8.9 0.7 convert_element_type.76
  9.6 9.4 %fusion.2 = bf16[3072,768]{0,1:T(8,128)(2,1)} fusion(bf16[1024,3072]{1,0:T(8,128)(2,1)} %param.7, bf16[1024,768]{1,0:T(8,128)(2,1)} %param.8, bf16[1024]{0:T(1024)(128)(2,1)S(1)} %convert_element_type.76), kind=kOutput, calls=%fused_computation.6 | convolution fusion | flops 4837343232 | bytes 12584960 | tf_op jit(solution)/shard_map/dot_general | solution.py:16
  19.0 6.7 %copy.24 = bf16[3072,768]{1,0:T(8,128)(2,1)} copy(bf16[3072,768]{0,1:T(8,128)(2,1)} %fusion.2) | data formatting | bytes 9437184 | tf_op jit(solution)/shard_map/convert_element_type | solution.py:69
  25.6 2.7 copy.25
  28.3 9.7 %all_to_all.42 = bf16[16,2,96,768]{3,2,0,1:T(8,128)(2,1)} all-to-all(bf16[16,2,96,768]{3,2,0,1:T(8,128)(2,1)S(1)} %copy.25), channel_id=1, replica_groups=mesh['pairs'=16,'core'=2,'fac'=4] {'core'}, dimensions={1} | all-to-all | bytes 9437184 | tf_op jit(solution)/shard_map/all_to_all | solution.py:47
  38.0 3.5 %reduce_sum.135 = bf16[16,96,768]{2,1,0:T(8,128)(2,1)S(1)} reduce(bf16[16,2,96,768]{3,2,0,1:T(8,128)(2,1)} %all_to_all.42, bf16[]{:T(256)} %constant.44.clone.1), dimensions={1}, to_apply=%region_0.0 | reduce | flops 1179648 | bytes 7077890 | tf_op jit(solution)/shard_map/reduce_sum | solution.py:48
  41.5 43.2 %all_to_all.43 = bf16[16,96,768]{2,1,0:T(8,128)(2,1)S(1)} all-to-all(bf16[16,96,768]{2,1,0:T(8,128)(2,1)S(1)} %reduce_sum.135), channel_id=1, replica_groups=mesh['pairs'=16,'core'=2,'fac'=4] {'pairs'}, dimensions={0} | all-to-all | bytes 4718592 | tf_op jit(solution)/shard_map/all_to_all | solution.py:49
  85.1 0.7 negate_convert_fusion
  85.9 6.2 %gather_fusion = f32[1024]{0:T(1024)S(1)} fusion(f32[32768]{0:T(1024)S(1)} %copy-done, s32[1024]{0:T(1024)S(1)} %fusion.19), kind=kCustom, calls=%fused_computation | custom fusion | bytes 12288 | tf_op jit(solution)/shard_map/gather | solution.py:65
  92.1 1.7 multiply_convert_fusion.1
  93.8 1.1 copy-done.2
  95.0 7.0 %fusion.3 = bf16[3072,384]{0,1:T(8,128)(2,1)} fusion(bf16[1024,3072]{1,0:T(8,128)(2,1)} %param.7, bf16[1024,768]{1,0:T(8,128)(2,1)S(1)} %multiply_convert_fusion.1), kind=kOutput, calls=%fused_computation.9 | convolution fusion | flops 2417098752 | bytes 9437184 | tf_op jit(solution)/shard_map/dot_general | solution.py:16
  101.9 3.0 copy.26
  105.2 6.1 %all_to_all.44 = bf16[16,2,96,384]{3,2,0,1:T(8,128)(2,1)S(1)} all-to-all(bf16[16,2,96,384]{3,2,0,1:T(8,128)(2,1)S(1)} %copy.27), channel_id=1, replica_groups=mesh['pairs'=16,'core'=2,'fac'=4] {'core'}, dimensions={1} | all-to-all | bytes 4718592 | tf_op jit(solution)/shard_map/all_to_all | solution.py:47
  111.3 1.8 reduce_sum.137
  113.1 30.0 %all_to_all.45 = bf16[16,96,384]{2,1,0:T(8,128)(2,1)S(1)} all-to-all(bf16[16,96,384]{2,1,0:T(8,128)(2,1)} %reduce_sum.137), channel_id=1, replica_groups=mesh['pairs'=16,'core'=2,'fac'=4] {'pairs'}, dimensions={0} | all-to-all | bytes 2359296 | tf_op jit(solution)/shard_map/all_to_all | solution.py:49
  143.2 2.0 all-gather.7.cloned.1.call-done
  145.3 3.2 fusion.15
  148.5 11.5 %all_gather.23 = bf16[96,3072]{1,0:T(8,128)(2,1)S(1)} all-gather(bf16[96,768]{1,0:T(8,128)(2,1)S(1)} %fusion.15), channel_id=1, replica_groups=mesh['pairs'=16,'core'=2,'fac'=4] {'fac'}, dimensions={1}, use_global_device_ids=true | all-gather | bytes 737280 | tf_op jit(solution)/shard_map/all_gather | solution.py:79
  160.0 3.9 %fusion.27 = (bf16[96,768]{1,0:T(8,128)(2,1)}, f32[96,768]{1,0:T(8,128)S(1)}) fusion(bf16[96,3072]{1,0:T(8,128)(2,1)S(1)} %all_gather.23, bf16[3072,768]{1,0:T(8,128)(2,1)} %param.13), kind=kOutput, calls=%fused_computation.59 | convolution fusion | flops 453058560 | bytes 5750784 | tf_op jit(solution)/shard_map/dot_general | solution.py:78
  163.9 6.8 %fusion.4 = bf16[3072,384]{0,1:T(8,128)(2,1)} fusion(bf16[1024,3072]{1,0:T(8,128)(2,1)} %param.7, bf16[1024,768]{1,0:T(8,128)(2,1)S(1)} %copy-done.3), kind=kOutput, calls=%fused_computation.10 | convolution fusion | flops 2417098752 | bytes 9437184 | tf_op jit(solution)/shard_map/dot_general | solution.py:16
  170.8 3.0 copy.28
  174.0 7.5 %all_to_all.46 = bf16[16,2,96,384]{3,2,0,1:T(8,128)(2,1)S(1)} all-to-all(bf16[16,2,96,384]{3,2,0,1:T(8,128)(2,1)S(1)} %copy.29), channel_id=1, replica_groups=mesh['pairs'=16,'core'=2,'fac'=4] {'core'}, dimensions={1} | all-to-all | bytes 4718592 | tf_op jit(solution)/shard_map/all_to_all | solution.py:47
  181.5 1.8 reduce_sum.140
  183.3 26.3 %all_to_all.47 = bf16[16,96,384]{2,1,0:T(8,128)(2,1)S(1)} all-to-all(bf16[16,96,384]{2,1,0:T(8,128)(2,1)} %reduce_sum.140), channel_id=1, replica_groups=mesh['pairs'=16,'core'=2,'fac'=4] {'pairs'}, dimensions={0} | all-to-all | bytes 2359296 | tf_op jit(solution)/shard_map/all_to_all | solution.py:49
  209.8 11.7 %all_gather.24 = bf16[96,3072]{1,0:T(8,128)(2,1)S(1)} all-gather(bf16[96,768]{1,0:T(8,128)(2,1)S(1)} %pad_maximum_fusion), channel_id=1, replica_groups=mesh['pairs'=16,'core'=2,'fac'=4] {'fac'}, dimensions={1}, use_global_device_ids=true | all-gather | bytes 737280 | tf_op jit(solution)/shard_map/all_gather | solution.py:110
  221.5 4.5 %multiply_reduce_fusion.5 = (f32[]{:T(128)}, f32[]{:T(128)}, bf16[96,768]{1,0:T(8,128)(2,1)}, f32[96,768]{1,0:T(8,128)S(1)}) fusion(f32[96,768]{1,0:T(8,128)S(1)} %get-tuple-element.26, f32[96,768]{1,0:T(8,128)S(1)} %convert_reduce_fusion, bf16[96,3072]{1,0:T(8,128)(2,1)S(1)} %all_gather.24, bf16[3072,768]{1,0:T(8,128)(2,1)} %all-gather.9.cloned.1.call-done), kind=kOutput, calls=%fused_computation.43 | convolution fusion | flops 453574656 | bytes 6340616 | tf_op jit(solution)/shard_map/dot_general | solution.py:12
  226.0 3.3 convolution_convert_fusion.3
  229.3 1.4 pad_maximum_fusion.1
  230.6 0.7 broadcast_in_dim.7
  231.3 10.9 %all-to-all-start.6 = ((f32[128,1,2]{2,1,0:T(1,128)}), f32[128,1,2]{2,1,0:T(1,128)S(1)}, u32[]{:S(2)}, u32[]{:S(2)}) async-start(f32[128,1,2]{2,1,0:T(1,128)} %broadcast_in_dim.7), calls=%async_computation.6 | async-start | bytes 131072 | tf_op jit(solution)/shard_map/all_to_all | solution.py:56
  242.2 11.3 %all_gather.26 = bf16[96,3072]{1,0:T(8,128)(2,1)S(1)} all-gather(bf16[96,768]{1,0:T(8,128)(2,1)S(1)} %convolution_convert_fusion.3), channel_id=1, replica_groups=mesh['pairs'=16,'core'=2,'fac'=4] {'fac'}, dimensions={1}, use_global_device_ids=true | all-gather | bytes 737280 | tf_op jit(solution)/shard_map/all_gather | solution.py:119
  255.7 20.6 %all-gather.11.cloned.1.call-done = bf16[3072,768]{1,0:T(8,128)(2,1)} async-done(((bf16[96,768]{1,0:T(8,128)(2,1)}), bf16[3072,768]{1,0:T(8,128)(2,1)}) %all-gather.11.cloned.1.call-update) | async-done | bytes 4718608 | tf_op jit(solution)/shard_map/all_gather | solution.py:73
  276.2 5.6 %fusion.6 = bf16[192,768]{1,0:T(8,128)(2,1)S(1)} fusion(bf16[3072,768]{1,0:T(8,128)(2,1)} %all-gather.11.cloned.1.call-done, bf16[3072,768]{1,0:T(8,128)(2,1)} %all-gather.7.cloned.1.call-done, f32[]{:T(128)S(6)} %div.17, bf16[96,3072]{1,0:T(8,128)(2,1)S(1)} %all_gather.26, bf16[96,3072]{1,0:T(8,128)(2,1)S(1)} %copy-done.5), kind=kOutput, calls=%fused_computation.18 | convolution fusion | flops 920272896 | bytes 10911748 | tf_op jit(solution)/shard_map/dot_general | solution.py:12
  281.8 1.3 collective-permute-start
  283.1 1.5 collective-permute-start.1
  284.6 1.7 fusion.13
  286.2 5.2 %collective-permute-done = bf16[192,768]{1,0:T(8,128)(2,1)S(1)} collective-permute-done((bf16[192,768]{1,0:T(8,128)(2,1)S(1)}, bf16[192,768]{1,0:T(8,128)(2,1)S(1)}, u32[]{:S(2)}, u32[]{:S(2)}) %collective-permute-start) | collective-permute-done | bytes 294944 | tf_op jit(solution)/shard_map/ppermute | solution.py:36
  291.4 1.7 convolution_add_fusion.2
  293.2 1.7 convolution_add_fusion.1
  294.9 5.2 %collective-permute-done.2 = bf16[192,768]{1,0:T(8,128)(2,1)S(1)} collective-permute-done((bf16[192,768]{1,0:T(8,128)(2,1)S(1)}, bf16[192,768]{1,0:T(8,128)(2,1)S(1)}, u32[]{:S(2)}, u32[]{:S(2)}) %collective-permute-start.2) | collective-permute-done | bytes 294944 | tf_op jit(solution)/shard_map/ppermute | solution.py:36
  300.1 1.7 convolution_add_fusion
  301.8 0.8 multiply_reduce_fusion.3
  302.6 2.5 pad_maximum_fusion.2
  305.2 16.0 %all_to_all.48 = f32[128,1,4]{2,1,0:T(1,128)S(1)} all-to-all(f32[128,1,4]{2,1,0:T(1,128)S(1)} %broadcast_in_dim.8), channel_id=1, replica_groups=mesh['pairs'=16,'core'=2,'fac'=4] {'pairs','core','fac'}, dimensions={0} | all-to-all | bytes 4096 | tf_op jit(solution)/shard_map/all_to_all | solution.py:56
  321.3 0.6 fusion.25
  326.4 1.0 multiply_subtract_fusion
  (40 shorter events, 2.4 us)
Async XLA Ops:
  7.2 78.7 %copy-start = (f32[32768]{0:T(1024)S(1)}, f32[32768]{0:T(1024)}, u32[]{:S(2)}) copy-start(f32[32768]{0:T(1024)} %param.11) | copy-start | bytes 393220
  7.2 77.9 %all-gather.5.cloned.1.call-start = ((), (), s32[]{:S(2)}) async-start(), calls=%async_computation.8 | async-start | bytes 4866048 | tf_op jit(solution)/shard_map/all_gather | solution.py:88
  8.8 136.4 %all-gather.7.cloned.1.call-start = ((), (), s32[]{:S(2)}) async-start(), calls=%async_computation.9 | async-start | bytes 4866048 | tf_op jit(solution)/shard_map/all_gather | solution.py:73
  41.5 44.3 %copy-start.7 = (s32[1024]{0:T(1024)S(1)}, s32[1024]{0:T(1024)}, u32[]{:S(2)}) copy-start(s32[1024]{0:T(1024)} %param.9) | copy-start | bytes 12292
  84.7 7.3 %copy-start.6 = (s32[1024]{0:T(1024)S(1)}, s32[1024]{0:T(1024)}, u32[]{:S(2)}) copy-start(s32[1024]{0:T(1024)} %param.10) | copy-start | bytes 12292
  85.8 135.7 %all-gather.9.cloned.1.call-start = ((), (), s32[]{:S(2)}) async-start(), calls=%async_computation.10 | async-start | bytes 4866048 | tf_op jit(solution)/shard_map/all_gather | solution.py:73
  93.8 1.1 copy-start.2
  111.3 34.0 %copy-start.4 = (bf16[96,3072]{1,0:T(8,128)(2,1)S(1)}, bf16[96,3072]{1,0:T(8,128)(2,1)}, u32[]{:S(2)}) copy-start(bf16[96,3072]{1,0:T(8,128)(2,1)} %param.12) | copy-start | bytes 1769476
  143.2 20.7 %copy-start.3 = (bf16[1024,768]{1,0:T(8,128)(2,1)S(1)}, bf16[1024,768]{1,0:T(8,128)(2,1)}, u32[]{:S(2)}) copy-start(bf16[1024,768]{1,0:T(8,128)(2,1)} %copy-done.2) | copy-start | bytes 4718596
  163.9 112.4 %all-gather.11.cloned.1.call-start = ((), (), s32[]{:S(2)}) async-start(), calls=%async_computation.11 | async-start | bytes 4866048 | tf_op jit(solution)/shard_map/all_gather | solution.py:73
  226.0 50.3 %copy-start.5 = (bf16[96,3072]{1,0:T(8,128)(2,1)S(1)}, bf16[96,3072]{1,0:T(8,128)(2,1)}, u32[]{:S(2)}) copy-start(bf16[96,3072]{1,0:T(8,128)(2,1)} %param.12) | copy-start | bytes 1769476
  231.3 22.2 %all-to-all-start.6 = ((f32[128,1,2]{2,1,0:T(1,128)}), f32[128,1,2]{2,1,0:T(1,128)S(1)}, u32[]{:S(2)}, u32[]{:S(2)}) async-start(f32[128,1,2]{2,1,0:T(1,128)} %broadcast_in_dim.7), calls=%async_computation.6 | async-start | bytes 131072 | tf_op jit(solution)/shard_map/all_to_all | solution.py:56
  281.8 9.6 %collective-permute-start = (bf16[192,768]{1,0:T(8,128)(2,1)S(1)}, bf16[192,768]{1,0:T(8,128)(2,1)S(1)}, u32[]{:S(2)}, u32[]{:S(2)}) collective-permute-start(bf16[192,768]{1,0:T(8,128)(2,1)S(1)} %fusion.6), channel_id=1, source_target_pairs={{0,1},{1,2},{2,3},{3,0},{4,5},{5,6},{6,7},{7,4},{8,9},{9,10},{10,1... | collective-permute-start | bytes 884744 | tf_op jit(solution)/shard_map/ppermute | solution.py:36
  283.1 10.1 %collective-permute-start.1 = (bf16[192,768]{1,0:T(8,128)(2,1)S(1)}, bf16[192,768]{1,0:T(8,128)(2,1)S(1)}, u32[]{:S(2)}, u32[]{:S(2)}) collective-permute-start(bf16[192,768]{1,0:T(8,128)(2,1)S(1)} %fusion.6), channel_id=1, source_target_pairs={{0,3},{1,0},{2,1},{3,2},{4,7},{5,4},{6,5},{7,6},{8,11},{9,8},{10,9... | collective-permute-start | bytes 884744 | tf_op jit(solution)/shard_map/ppermute | solution.py:39
  291.4 8.6 %collective-permute-start.2 = (bf16[192,768]{1,0:T(8,128)(2,1)S(1)}, bf16[192,768]{1,0:T(8,128)(2,1)S(1)}, u32[]{:S(2)}, u32[]{:S(2)}) collective-permute-start(bf16[192,768]{1,0:T(8,128)(2,1)S(1)} %collective-permute-done), channel_id=1, source_target_pairs={{0,1},{1,2},{2,3},{3,0},{4,5},{5,6},{6,7},{7,4},{8,9},{9,10},{10,1... | collective-permute-start | bytes 884744 | tf_op jit(solution)/shard_map/ppermute | solution.py:36
  291.4 35.9 %copy-start.1 = (f32[32768]{0:T(1024)S(1)}, f32[32768]{0:T(1024)}, u32[]{:S(2)}) copy-start(f32[32768]{0:T(1024)} %param.11) | copy-start | bytes 393220
Sparse Core Ops, SparseCore 0:
  10.8 68.8 all-gather.4
  85.9 59.2 all-gather.6
  164.0 53.3 all-gather.8
  226.1 50.0 all-gather.10
where the time goes:
time: 335 us; the launch traced here: 334 us
  blocking collectives  173 us (52%)
  matrix products  50.4 us (15%)
  waiting for transfers between devices  33.1 us (10%)
  local copies, waits for them, and re-layouts  26.6 us (8%)
  between operations  19.9 us (6%)
  other arithmetic  16.8 us (5%)
  starting transfers between devices  13.8 us (4%)
    all_to_all x3, blocking collectives, scatter_sum(): received = lax.all_to_all(chip_sum, 'pairs', 0, 0, tiled=False)  99.5 us
    all_to_all x3, blocking collectives, scatter_sum(): on_chip = lax.all_to_all(blocks, 'core', 1, 1, tiled=False)  23.4 us
    dot_general x8, matrix products, add_columns(): return jnp.dot(matrix, piece, preferred_element_type=jnp.float32)  23.3 us
    dot_general x3, matrix products, transposed_term(): lax.dot_general(matrix, right, (((0,), (0,)), ((), ())), preferred_elemen...  23.2 us
    all_gather x3, waiting for transfers between devices, gather_rows(): return lax.all_gather(matrix.astype(jnp.bfloat16), FSDP, axis=0, tiled=True)  22.6 us
    all_to_all x1, blocking collectives, global_sums(): received = lax.all_to_all(stacked, FSDP + ('fac',), 0, 0, tiled=True)  16 us
    all_gather x1, blocking collectives, body(): lax.all_gather(gram_own.astype(jnp.bfloat16), 'fac', axis=1, tiled=True)  11.7 us
    all_gather x1, blocking collectives, precondition(): lax.all_gather(mixed_low, 'fac', axis=1, tiled=True)  11.5 us
  transfers between devices with their start and end apart: 8, of which 4 were waited for; matrix products, arithmetic and copies ran while one was open for 20% of the time, Pallas kernels for 0%

commit v1 on v0

--- a/solution.py
+++ b/solution.py
@@ -70,7 +70,12 @@
     )
 
     def gather_rows(matrix):
-        return lax.all_gather(matrix.astype(jnp.bfloat16), FSDP, axis=0, tiled=True)
+        return jnp.concatenate(
+            lax.all_to_all(
+                jnp.stack([matrix.astype(jnp.bfloat16)] * lax.axis_size(FSDP)), FSDP, 0, 0
+            ),
+            axis=0,
+        )
 
     def precondition(gathered):
         mixed = add_columns(in_inverse, gathered)

time: 335 us -> 472 us (1.41)
  waiting for transfers between devices: 33.1 us -> 191 us
  blocking collectives: 173 us -> 81.3 us
  starting transfers between devices: 13.8 us -> 56.6 us
  other arithmetic: 16.8 us -> 33.4 us
  local copies, waits for them, and re-layouts: 26.6 us -> 39.8 us
    all_to_all x1 -> x8, waiting for transfers between devices: 0.01 us -> 184 us  [the longest x3 137 us: gather_rows(): lax.all_to_all(jnp.stack([matrix.astype(jnp.bfloat16)] * lax.axis_size(FS...]
    all_to_all x3 -> x0, blocking collectives: 99.5 us -> none  [scatter_sum(): received = lax.all_to_all(chip_sum, 'pairs', 0, 0, tiled=False)]
    all_to_all x1 -> x8, starting transfers between devices: 10.9 us -> 53.8 us  [the longest x3 24.5 us: gather_rows(): lax.all_to_all(jnp.stack([matrix.astype(jnp.bfloat16)] * lax.axis_size(FS...]
    all_gather x3 -> x0, waiting for transfers between devices: 22.6 us -> none  [gather_rows(): return lax.all_gather(matrix.astype(jnp.bfloat16), FSDP, axis=0, tiled=True)]
    all_to_all x1 -> x2, blocking collectives: 16 us -> 37.6 us  [global_sums(): received = lax.all_to_all(stacked, FSDP + ('fac',), 0, 0, tiled=True)]
    all_to_all x3 -> x1, blocking collectives: 23.4 us -> 8.87 us  [scatter_sum(): on_chip = lax.all_to_all(blocks, 'core', 1, 1, tiled=False)]
    another operation x0 -> x3, local copies, waits for them, and re-layouts: none -> 8.1 us  [gather_rows(): jnp.stack([matrix.astype(jnp.bfloat16)] * lax.axis_size(FSDP))]
    convert_element_type x1 -> x2, other arithmetic: 0.68 us -> 7.03 us  [the longest x1 7.01 us: body(): (residual_rows.astype(jnp.float32) - alpha * image_rows.astype(jnp.float3...]
  transfers between devices with their start and end apart: 8 -> 12, of which waited for: 4 -> 7; matrix products, arithmetic and copies ran while one was open for 20% -> 18% of each run, Pallas kernels for 0% -> 0%
where the time goes in v1:
time: 472 us; the launch traced here: 470 us
  waiting for transfers between devices  191 us (40%)
  blocking collectives  81.3 us (17%)
  starting transfers between devices  56.6 us (12%)
  matrix products  47.9 us (10%)
  local copies, waits for them, and re-layouts  39.8 us (8%)
  other arithmetic  33.4 us (7%)
  between operations  20.1 us (4%)
    all_to_all x3, waiting for transfers between devices, gather_rows(): lax.all_to_all(jnp.stack([matrix.astype(jnp.bfloat16)] * lax.axis_size(FS...  137 us
    all_to_all x3, waiting for transfers between devices, scatter_sum(): received = lax.all_to_all(chip_sum, 'pairs', 0, 0, tiled=False)  47.5 us
    all_to_all x2, blocking collectives, global_sums(): received = lax.all_to_all(stacked, FSDP + ('fac',), 0, 0, tiled=True)  37.6 us
    all_to_all x3, starting transfers between devices, gather_rows(): lax.all_to_all(jnp.stack([matrix.astype(jnp.bfloat16)] * lax.axis_size(FS...  24.5 us
    dot_general x3, matrix products, transposed_term(): lax.dot_general(matrix, right, (((0,), (0,)), ((), ())), preferred_elemen...  23.1 us
    dot_general x8, matrix products, add_columns(): return jnp.dot(matrix, piece, preferred_element_type=jnp.float32)  21.6 us
    all_to_all x3, starting transfers between devices, scatter_sum(): received = lax.all_to_all(chip_sum, 'pairs', 0, 0, tiled=False)  17.9 us
    all_gather x1, blocking collectives, body(): lax.all_gather(add_columns(gram_rows, in_cols).astype(jnp.bfloat16), 'fac...  11.9 us
  transfers between devices with their start and end apart: 12, of which 7 were waited for; matrix products, arithmetic and copies ran while one was open for 18% of the time, Pallas kernels for 0%

profile of v1, /device:TPU:1, one launch (start us, length us, event | category | flops | bytes accessed | tf_op | source)
XLA Modules:
  0.0 470.5 jit_solution(18277999471938959987)
XLA Ops:
  9.5 9.3 %fusion.1 = bf16[3072,768]{0,1:T(8,128)(2,1)} fusion(bf16[1024,3072]{1,0:T(8,128)(2,1)} %param.7, bf16[1024,768]{1,0:T(8,128)(2,1)} %param.8, bf16[1024]{0:T(1024)(128)(2,1)S(1)} %convert_element_type.77), kind=kOutput, calls=%fused_computation.6 | convolution fusion | flops 4837343232 | bytes 12584960 | tf_op jit(solution)/shard_map/dot_general | solution.py:16
  18.9 6.7 %copy.24 = bf16[3072,768]{1,0:T(8,128)(2,1)} copy(bf16[3072,768]{0,1:T(8,128)(2,1)} %fusion.1) | data formatting | bytes 9437184 | tf_op jit(solution)/shard_map/convert_element_type | solution.py:69
  25.6 4.9 %copy.25 = bf16[16,2,96,768]{3,2,0,1:T(8,128)(2,1)} copy(bf16[16,2,96,768]{3,2,1,0:T(8,128)(2,1)} %bitcast.44) | data formatting | bytes 9437184 | tf_op jit(solution)/shard_map/reshape | solution.py:46
  30.5 7.4 %all-to-all-start = ((bf16[16,2,96,768]{3,2,0,1:T(8,128)(2,1)}), bf16[16,2,96,768]{3,2,0,1:T(8,128)(2,1)}, u32[]{:S(2)}, u32[]{:S(2)}) async-start(bf16[16,2,96,768]{3,2,0,1:T(8,128)(2,1)} %copy.25), calls=%async_computation | async-start | bytes 9437184 | tf_op jit(solution)/shard_map/all_to_all | solution.py:47
  37.9 6.2 %gather_fusion = f32[1024]{0:T(1024)S(1)} fusion(f32[32768]{0:T(1024)S(1)} %copy-done, s32[1024]{0:T(1024)S(1)} %fusion.17), kind=kCustom, calls=%fused_computation | custom fusion | bytes 12288 | tf_op jit(solution)/shard_map/gather | solution.py:65
  44.1 1.8 multiply_convert_fusion.1
  47.0 6.9 %fusion.3 = bf16[3072,384]{0,1:T(8,128)(2,1)} fusion(bf16[1024,3072]{1,0:T(8,128)(2,1)} %param.7, bf16[1024,768]{1,0:T(8,128)(2,1)S(1)} %multiply_convert_fusion.1), kind=kOutput, calls=%fused_computation.10 | convolution fusion | flops 2417098752 | bytes 9437184 | tf_op jit(solution)/shard_map/dot_general | solution.py:16
  54.0 3.0 copy.28
  59.1 6.9 %fusion.2 = bf16[3072,384]{0,1:T(8,128)(2,1)} fusion(bf16[1024,3072]{1,0:T(8,128)(2,1)} %param.7, bf16[1024,768]{1,0:T(8,128)(2,1)S(1)} %copy-done.6), kind=kOutput, calls=%fused_computation.9 | convolution fusion | flops 2417098752 | bytes 9437184 | tf_op jit(solution)/shard_map/dot_general | solution.py:16
  65.9 3.0 copy.26
  68.9 1.7 copy.27
  70.6 4.1 all-to-all-start.5
  74.8 5.4 %reduce_sum.135 = bf16[16,96,768]{2,1,0:T(8,128)(2,1)} reduce(bf16[16,2,96,768]{3,2,0,1:T(8,128)(2,1)} %all-to-all-done, bf16[]{:T(256)} %constant.44.clone.1), dimensions={1}, to_apply=%region_0.0 | reduce | flops 1179648 | bytes 7077890 | tf_op jit(solution)/shard_map/reduce_sum | solution.py:48
  80.2 8.9 %all_to_all.57 = bf16[16,2,96,384]{3,2,0,1:T(8,128)(2,1)} all-to-all(bf16[16,2,96,384]{3,2,0,1:T(8,128)(2,1)} %copy.27), channel_id=1, replica_groups=mesh['pairs'=16,'core'=2,'fac'=4] {'core'}, dimensions={1} | all-to-all | bytes 4718592 | tf_op jit(solution)/shard_map/all_to_all | solution.py:47
  89.1 7.5 %all-to-all-start.1 = ((bf16[16,96,768]{2,1,0:T(8,128)(2,1)}), bf16[16,96,768]{2,1,0:T(8,128)(2,1)}, u32[]{:S(2)}, u32[]{:S(2)}) async-start(bf16[16,96,768]{2,1,0:T(8,128)(2,1)} %reduce_sum.135), calls=%async_computation.1 | async-start | bytes 4718592 | tf_op jit(solution)/shard_map/all_to_all | solution.py:49
  96.6 3.4 reduce_sum.137
  100.0 32.7 %all-to-all-done.1 = bf16[16,96,768]{2,1,0:T(8,128)(2,1)} async-done(((bf16[16,96,768]{2,1,0:T(8,128)(2,1)}), bf16[16,96,768]{2,1,0:T(8,128)(2,1)}, u32[]{:S(2)}, u32[]{:S(2)}) %all-to-all-start.1) | async-done | bytes 2359328 | tf_op jit(solution)/shard_map/all_to_all | solution.py:49
  132.7 4.4 all-to-all-start.4
  137.1 2.0 convert_reduce_fusion
  139.1 14.8 %all-to-all-done.4 = bf16[16,96,384]{2,1,0:T(8,128)(2,1)} async-done(((bf16[16,96,384]{2,1,0:T(8,128)(2,1)}), bf16[16,96,384]{2,1,0:T(8,128)(2,1)}, u32[]{:S(2)}, u32[]{:S(2)}) %all-to-all-start.4) | async-done | bytes 1179680 | tf_op jit(solution)/shard_map/all_to_all | solution.py:49
  153.9 2.8 stack.22
  156.7 7.7 %all-to-all-start.2 = ((bf16[32,96,768]{2,1,0:T(8,128)(2,1)}), bf16[32,96,768]{2,1,0:T(8,128)(2,1)}, u32[]{:S(2)}, u32[]{:S(2)}) async-start(bf16[32,96,768]{2,1,0:T(8,128)(2,1)} %stack.22), calls=%async_computation.2 | async-start | bytes 9437184 | tf_op jit(solution)/shard_map/all_to_all | solution.py:74
  164.4 1.8 reduce_sum.140
  166.2 54.0 %all-to-all-done.2 = bf16[32,96,768]{2,1,0:T(8,128)(2,1)} async-done(((bf16[32,96,768]{2,1,0:T(8,128)(2,1)}), bf16[32,96,768]{2,1,0:T(8,128)(2,1)}, u32[]{:S(2)}, u32[]{:S(2)}) %all-to-all-start.2) | async-done | bytes 4718624 | tf_op jit(solution)/shard_map/all_to_all | solution.py:74
  220.2 6.0 %all-to-all-start.6 = ((bf16[16,96,384]{2,1,0:T(8,128)(2,1)}), bf16[16,96,384]{2,1,0:T(8,128)(2,1)S(1)}, u32[]{:S(2)}, u32[]{:S(2)}) async-start(bf16[16,96,384]{2,1,0:T(8,128)(2,1)} %reduce_sum.140), calls=%async_computation.6 | async-start | bytes 2359296 | tf_op jit(solution)/shard_map/all_to_all | solution.py:49
  227.6 3.2 fusion.13
  230.8 11.6 %all_gather.13 = bf16[96,3072]{1,0:T(8,128)(2,1)S(1)} all-gather(bf16[96,768]{1,0:T(8,128)(2,1)S(1)} %fusion.13), channel_id=1, replica_groups=mesh['pairs'=16,'core'=2,'fac'=4] {'fac'}, dimensions={1}, use_global_device_ids=true | all-gather | bytes 737280 | tf_op jit(solution)/shard_map/all_gather | solution.py:84
  242.5 3.2 fusion.25
  245.7 2.7 stack.24
  248.4 11.7 %all-to-all-start.7 = ((bf16[32,96,768]{2,1,0:T(8,128)(2,1)}), bf16[32,96,768]{2,1,0:T(8,128)(2,1)}, u32[]{:S(2)}, u32[]{:S(2)}) async-start(bf16[32,96,768]{2,1,0:T(8,128)(2,1)} %stack.24), calls=%async_computation.7 | async-start | bytes 9437184 | tf_op jit(solution)/shard_map/all_to_all | solution.py:74
  260.2 11.3 %all_gather.14 = bf16[96,3072]{1,0:T(8,128)(2,1)S(1)} all-gather(bf16[96,768]{1,0:T(8,128)(2,1)S(1)} %pad_maximum_fusion), channel_id=1, replica_groups=mesh['pairs'=16,'core'=2,'fac'=4] {'fac'}, dimensions={1}, use_global_device_ids=true | all-gather | bytes 737280 | tf_op jit(solution)/shard_map/all_gather | solution.py:115
  271.5 44.3 %all-to-all-done.7 = bf16[32,96,768]{2,1,0:T(8,128)(2,1)} async-done(((bf16[32,96,768]{2,1,0:T(8,128)(2,1)}), bf16[32,96,768]{2,1,0:T(8,128)(2,1)}, u32[]{:S(2)}, u32[]{:S(2)}) %all-to-all-start.7) | async-done | bytes 4718624 | tf_op jit(solution)/shard_map/all_to_all | solution.py:74
  315.8 4.6 multiply_reduce_fusion.5
  321.8 16.9 %all_to_all.58 = f32[128,1,2]{2,1,0:T(1,128)S(1)} all-to-all(f32[128,1,2]{2,1,0:T(1,128)S(1)} %broadcast_in_dim.7), channel_id=1, replica_groups=mesh['pairs'=16,'core'=2,'fac'=4] {'pairs','core','fac'}, dimensions={0} | all-to-all | bytes 2048 | tf_op jit(solution)/shard_map/all_to_all | solution.py:56
  338.6 2.7 stack.27
  341.3 5.1 %all-to-all-start.9 = ((bf16[32,96,768]{2,1,0:T(8,128)(2,1)}), bf16[32,96,768]{2,1,0:T(8,128)(2,1)}, u32[]{:S(2)}, u32[]{:S(2)}) async-start(bf16[32,96,768]{2,1,0:T(8,128)(2,1)} %stack.27), calls=%async_computation.9 | async-start | bytes 9437184 | tf_op jit(solution)/shard_map/all_to_all | solution.py:74
  346.5 3.2 convolution_convert_fusion.4
  349.7 11.9 %all_gather.15 = bf16[96,3072]{1,0:T(8,128)(2,1)} all-gather(bf16[96,768]{1,0:T(8,128)(2,1)S(1)} %convolution_convert_fusion.4), channel_id=1, replica_groups=mesh['pairs'=16,'core'=2,'fac'=4] {'fac'}, dimensions={1}, use_global_device_ids=true | all-gather | bytes 737280 | tf_op jit(solution)/shard_map/all_gather | solution.py:124
  363.7 38.6 %all-to-all-done.9 = bf16[32,96,768]{2,1,0:T(8,128)(2,1)} async-done(((bf16[32,96,768]{2,1,0:T(8,128)(2,1)}), bf16[32,96,768]{2,1,0:T(8,128)(2,1)}, u32[]{:S(2)}, u32[]{:S(2)}) %all-to-all-start.9) | async-done | bytes 4718624 | tf_op jit(solution)/shard_map/all_to_all | solution.py:74
  402.3 3.5 convert_multiply_fusion
  405.8 7.0 %fusion = bf16[3072,768]{1,0:T(8,128)(2,1)} fusion(f32[32,96,768]{2,1,0:T(8,128)S(1)} %convert_multiply_fusion, bf16[3072,768]{1,0:T(8,128)(2,1)} %bitcast.2), kind=kLoop, calls=%fused_computation.2 | loop fusion | flops 7077888 | bytes 18874368 | tf_op jit(solution)/shard_map/convert_element_type | solution.py:130
  412.8 3.8 convolution_convert_fusion.2
  417.0 2.4 collective-permute-start.1
  421.0 2.4 collective-permute-done
  423.5 1.7 convolution_add_fusion.2
  426.9 4.5 collective-permute-done.2
  433.9 2.6 pad_maximum_fusion.2
  436.6 20.8 %all_to_all.59 = f32[128,1,4]{2,1,0:T(1,128)S(1)} all-to-all(f32[128,1,4]{2,1,0:T(1,128)S(1)} %broadcast_in_dim.8), channel_id=1, replica_groups=mesh['pairs'=16,'core'=2,'fac'=4] {'pairs','core','fac'}, dimensions={0} | all-to-all | bytes 4096 | tf_op jit(solution)/shard_map/all_to_all | solution.py:56
  (50 shorter events, 17.4 us)
Async XLA Ops:
  7.2 30.7 %copy-start = (f32[32768]{0:T(1024)S(1)}, f32[32768]{0:T(1024)}, u32[]{:S(2)}) copy-start(f32[32768]{0:T(1024)} %param.11) | copy-start | bytes 393220
  7.2 131.9 %all-gather.2.cloned.1.call-start = ((), (), s32[]{:S(2)}) async-start(), calls=%async_computation.11 | async-start | bytes 4866048 | tf_op jit(solution)/shard_map/all_gather | solution.py:93
  30.5 7.4 %copy-start.9 = (s32[1024]{0:T(1024)S(1)}, s32[1024]{0:T(1024)}, u32[]{:S(2)}) copy-start(s32[1024]{0:T(1024)} %param.9) | copy-start | bytes 12292
  30.5 13.5 %copy-start.8 = (s32[1024]{0:T(1024)S(1)}, s32[1024]{0:T(1024)}, u32[]{:S(2)}) copy-start(s32[1024]{0:T(1024)} %param.10) | copy-start | bytes 12292
  30.5 40.1 %all-to-all-start = ((bf16[16,2,96,768]{3,2,0,1:T(8,128)(2,1)}), bf16[16,2,96,768]{3,2,0,1:T(8,128)(2,1)}, u32[]{:S(2)}, u32[]{:S(2)}) async-start(bf16[16,2,96,768]{3,2,0,1:T(8,128)(2,1)} %copy.25), calls=%async_computation | async-start | bytes 9437184 | tf_op jit(solution)/shard_map/all_to_all | solution.py:47
  45.9 1.1 copy-start.5
  57.0 2.1 copy-start.6
  70.6 9.6 %all-to-all-start.5 = ((bf16[16,2,96,384]{3,2,0,1:T(8,128)(2,1)}), bf16[16,2,96,384]{3,2,0,1:T(8,128)(2,1)S(1)}, u32[]{:S(2)}, u32[]{:S(2)}) async-start(bf16[16,2,96,384]{3,2,0,1:T(8,128)(2,1)} %copy.29), calls=%async_computation.5 | async-start | bytes 4718592 | tf_op jit(solution)/shard_map/all_to_all | solution.py:47
  89.1 43.6 %all-to-all-start.1 = ((bf16[16,96,768]{2,1,0:T(8,128)(2,1)}), bf16[16,96,768]{2,1,0:T(8,128)(2,1)}, u32[]{:S(2)}, u32[]{:S(2)}) async-start(bf16[16,96,768]{2,1,0:T(8,128)(2,1)} %reduce_sum.135), calls=%async_computation.1 | async-start | bytes 4718592 | tf_op jit(solution)/shard_map/all_to_all | solution.py:49
  132.7 21.3 %all-to-all-start.4 = ((bf16[16,96,384]{2,1,0:T(8,128)(2,1)}), bf16[16,96,384]{2,1,0:T(8,128)(2,1)}, u32[]{:S(2)}, u32[]{:S(2)}) async-start(bf16[16,96,384]{2,1,0:T(8,128)(2,1)} %reduce_sum.137), calls=%async_computation.4 | async-start | bytes 2359296 | tf_op jit(solution)/shard_map/all_to_all | solution.py:49
  156.7 63.5 %all-to-all-start.2 = ((bf16[32,96,768]{2,1,0:T(8,128)(2,1)}), bf16[32,96,768]{2,1,0:T(8,128)(2,1)}, u32[]{:S(2)}, u32[]{:S(2)}) async-start(bf16[32,96,768]{2,1,0:T(8,128)(2,1)} %stack.22), calls=%async_computation.2 | async-start | bytes 9437184 | tf_op jit(solution)/shard_map/all_to_all | solution.py:74
  164.4 63.2 %copy-start.7 = (bf16[96,3072]{1,0:T(8,128)(2,1)S(1)}, bf16[96,3072]{1,0:T(8,128)(2,1)}, u32[]{:S(2)}) copy-start(bf16[96,3072]{1,0:T(8,128)(2,1)} %param.12) | copy-start | bytes 1769476
  220.2 25.5 %all-to-all-start.6 = ((bf16[16,96,384]{2,1,0:T(8,128)(2,1)}), bf16[16,96,384]{2,1,0:T(8,128)(2,1)S(1)}, u32[]{:S(2)}, u32[]{:S(2)}) async-start(bf16[16,96,384]{2,1,0:T(8,128)(2,1)} %reduce_sum.140), calls=%async_computation.6 | async-start | bytes 2359296 | tf_op jit(solution)/shard_map/all_to_all | solution.py:49
  245.7 70.1 %copy-start.2 = (f32[96,768]{1,0:T(8,128)}, f32[96,768]{1,0:T(8,128)S(1)}, u32[]{:S(2)}) copy-start(f32[96,768]{1,0:T(8,128)S(1)} %get-tuple-element.26) | copy-start | bytes 884740
  248.4 67.5 %all-to-all-start.7 = ((bf16[32,96,768]{2,1,0:T(8,128)(2,1)}), bf16[32,96,768]{2,1,0:T(8,128)(2,1)}, u32[]{:S(2)}, u32[]{:S(2)}) async-start(bf16[32,96,768]{2,1,0:T(8,128)(2,1)} %stack.24), calls=%async_computation.7 | async-start | bytes 9437184 | tf_op jit(solution)/shard_map/all_to_all | solution.py:74
  341.3 61.0 %all-to-all-start.9 = ((bf16[32,96,768]{2,1,0:T(8,128)(2,1)}), bf16[32,96,768]{2,1,0:T(8,128)(2,1)}, u32[]{:S(2)}, u32[]{:S(2)}) async-start(bf16[32,96,768]{2,1,0:T(8,128)(2,1)} %stack.27), calls=%async_computation.9 | async-start | bytes 9437184 | tf_op jit(solution)/shard_map/all_to_all | solution.py:74
  416.6 6.9 %collective-permute-start = (bf16[192,768]{1,0:T(8,128)(2,1)S(1)}, bf16[192,768]{1,0:T(8,128)(2,1)S(1)}, u32[]{:S(2)}, u32[]{:S(2)}) collective-permute-start(bf16[192,768]{1,0:T(8,128)(2,1)S(1)} %convolution_convert_fusion.2), channel_id=1, source_target_pairs={{0,1},{1,2},{2,3},{3,0},{4,5},{5,6},{6,7},{7,4},{8,9},{9,10},{10,1... | collective-permute-start | bytes 884744 | tf_op jit(solution)/shard_map/ppermute | solution.py:36
  417.0 16.1 %copy-start.3 = (f32[96,768]{1,0:T(8,128)S(1)}, f32[96,768]{1,0:T(8,128)}, u32[]{:S(2)}) copy-start(f32[96,768]{1,0:T(8,128)} %copy-done.2) | copy-start | bytes 884740
  417.0 16.1 %copy-start.4 = (f32[96,768]{1,0:T(8,128)S(1)}, f32[96,768]{1,0:T(8,128)}, u32[]{:S(2)}) copy-start(f32[96,768]{1,0:T(8,128)} %get-tuple-element.27) | copy-start | bytes 884740
  417.0 8.2 %collective-permute-start.1 = (bf16[192,768]{1,0:T(8,128)(2,1)S(1)}, bf16[192,768]{1,0:T(8,128)(2,1)S(1)}, u32[]{:S(2)}, u32[]{:S(2)}) collective-permute-start(bf16[192,768]{1,0:T(8,128)(2,1)S(1)} %convolution_convert_fusion.2), channel_id=1, source_target_pairs={{0,3},{1,0},{2,1},{3,2},{4,7},{5,4},{6,5},{7,6},{8,11},{9,8},{10,9... | collective-permute-start | bytes 884744 | tf_op jit(solution)/shard_map/ppermute | solution.py:39
  423.5 7.9 %collective-permute-start.2 = (bf16[192,768]{1,0:T(8,128)(2,1)S(1)}, bf16[192,768]{1,0:T(8,128)(2,1)S(1)}, u32[]{:S(2)}, u32[]{:S(2)}) collective-permute-start(bf16[192,768]{1,0:T(8,128)(2,1)S(1)} %collective-permute-done), channel_id=1, source_target_pairs={{0,1},{1,2},{2,3},{3,0},{4,5},{5,6},{6,7},{7,4},{8,9},{9,10},{10,1... | collective-permute-start | bytes 884744 | tf_op jit(solution)/shard_map/ppermute | solution.py:36
  423.5 40.1 %copy-start.1 = (f32[32768]{0:T(1024)S(1)}, f32[32768]{0:T(1024)}, u32[]{:S(2)}) copy-start(f32[32768]{0:T(1024)} %param.11) | copy-start | bytes 393220
Sparse Core Ops, SparseCore 0:
  10.8 50.6 all-gather.1
